TPU v7x, 256 devices: a whole 4x4x8 slice. The times are simulated.
256 devices in a mesh: expert: 8 (over z), mp: 32 (over x, y, core).
Axes of the slice: x: 4, y: 4, z: 8, core: 2. Of those that a mesh axis runs over, the one named last changes fastest.
Arguments:
- tokens: bfloat16 [4096, 2048], P('expert', 'mp'), may hold values from -6 to 6
- expert_route: int32 [4096, 2], P('expert'), may hold values from 0 to 7, all different within a row; in each aligned block of 512 rows (0 to 511, 512 to 1023, ...) at most 256 rows name the same one
- route_gate: float32 [4096, 2], P('expert'), may hold values from 0.05 to 1
- request_lengths: int32 [32], replicated, may hold values from 1 to 1024, 4096 in all
- request_adapter: int32 [32], replicated, may hold values from 0 to 63, as said below
- request_order: int32 [32], replicated, may hold values from 0 to 31, each once
- gate_weight: bfloat16 [8, 5632, 2048], P('expert', 'mp'), may hold values from -0.125 to 0.125
- up_weight: bfloat16 [8, 5632, 2048], P('expert', 'mp'), may hold values from -0.125 to 0.125
- down_weight: bfloat16 [8, 5632, 2048], P('expert', 'mp'), may hold values from -0.15625 to 0.15625
- adapter_in: bfloat16 [8, 1024, 2048], P('expert', 'mp'), may hold values from -0.125 to 0.125
- adapter_out: bfloat16 [8, 5632, 1024], P('expert', 'mp'), may hold values from -1.5 to 1.5
Outputs:
- mixed: bfloat16 [4096, 2048], P('expert', 'mp')
Inputs may be any that keep to these rules, and one draw needn't show every extreme that they name: `expert_route`: the two entries of a row differ; within each aligned block of 512 rows (the tokens held at one position along `expert`) no expert is named by more than 256 rows, and in some block some expert is named by exactly 256 rows. `request_lengths`: they sum to 4096; the largest is 1024. `request_order`: each request index appears once. `request_adapter`: exactly 16 different adapters appear.
All inputs are finite; a program needn't handle non-finite values.
Results may differ from a plain program's by a relative error of at most 0.035.
Values may be sent and summed in bfloat16 or wider, within the bound.
No kernel may reach another device: no remote copies, remote signals or barrier semaphores. Data moves between devices by JAX's collectives and lax.ppermute only.
A program may use at most 64 MiB of HBM per device.

v0:
```python
import jax
import jax.numpy as jnp
from jax import lax
from jax.sharding import PartitionSpec as P

RANK = 16
ADAPTERS = 64


def token_adapters(request_lengths, request_adapter, request_order, first_token, token_count):
    request_ids = jnp.arange(request_lengths.shape[0], dtype=jnp.int32)
    chosen = (request_order[:, None] == request_ids[None, :]).astype(jnp.int32)
    packed_lengths = jnp.sum(chosen * request_lengths[None, :], axis=1, dtype=jnp.int32)
    packed_adapters = jnp.sum(chosen * request_adapter[None, :], axis=1, dtype=jnp.int32)
    boundary = jnp.cumsum(packed_lengths, dtype=jnp.int32)
    positions = first_token + jnp.arange(token_count, dtype=jnp.int32)
    packed_index = jnp.sum(
        (boundary[None, :] <= positions[:, None]).astype(jnp.int32), axis=1, dtype=jnp.int32
    )
    matches = (packed_index[:, None] == request_ids[None, :]).astype(jnp.int32)
    return jnp.sum(matches * packed_adapters[None, :], axis=1, dtype=jnp.int32)


def expert_slots(routes, groups, capacity):
    flat_routes = routes.reshape(-1)
    one_hot = (flat_routes[:, None] == jnp.arange(groups, dtype=jnp.int32)[None, :]).astype(
        jnp.int32
    )
    before = jnp.cumsum(one_hot, axis=0, dtype=jnp.int32) - one_hot
    seat_index = jnp.sum(before * one_hot, axis=1, dtype=jnp.int32)
    return (flat_routes * capacity + seat_index).reshape(routes.shape)


def contract_last(left, right):
    return lax.dot_general(
        left, right, (((1,), (1,)), ((), ())), preferred_element_type=jnp.float32
    )


def on_device(
    tokens,
    expert_route,
    route_gate,
    request_lengths,
    request_adapter,
    request_order,
    gate_weight,
    up_weight,
    down_weight,
    adapter_in,
    adapter_out,
):
    tok_rows, local_feat = tokens.shape
    groups = lax.axis_size("expert")
    n_mp = lax.axis_size("mp")
    capacity = 4 * tok_rows // groups
    total_slots = groups * capacity
    source_group = lax.axis_index("expert")
    rank_w = adapter_in[0]
    rank_cols_w = lax.all_to_all(rank_w, "mp", split_axis=1, concat_axis=0, tiled=True)
    adapter_of = token_adapters(
        request_lengths, request_adapter, request_order, source_group * tok_rows, tok_rows
    )
    slot_index = expert_slots(expert_route, groups, capacity)
    flat_slots = slot_index.reshape(-1)
    flat_tokens = jnp.broadcast_to(
        jnp.arange(tok_rows, dtype=jnp.int32)[:, None], slot_index.shape
    ).reshape(-1)
    slot_token = jnp.zeros((total_slots,), jnp.int32).at[flat_slots].set(flat_tokens)
    filled = jnp.zeros((total_slots,), jnp.bool_).at[flat_slots].set(True)
    slot_adapter = jnp.where(filled, adapter_of[slot_token], -1)
    blank = jnp.zeros((), tokens.dtype)
    send_rows = jnp.where(filled[:, None], tokens[slot_token], blank)
    arrived_local = lax.all_to_all(send_rows, "expert", split_axis=0, concat_axis=0, tiled=True)
    arrived_adapter = lax.all_to_all(
        slot_adapter, "expert", split_axis=0, concat_axis=0, tiled=True
    )
    row_count = arrived_local.shape[0]
    part_all = contract_last(arrived_local, rank_cols_w)
    pick = (arrived_adapter[:, None] == jnp.arange(ADAPTERS, dtype=jnp.int32)[None, :]).astype(
        jnp.float32
    )
    part_rank = jnp.sum(part_all.reshape(row_count, ADAPTERS, RANK) * pick[:, :, None], axis=1)
    arrived = lax.all_gather(arrived_local, "mp", axis=1, tiled=True)
    parts = lax.all_gather(part_rank.astype(jnp.bfloat16), "mp", axis=0, tiled=False)
    rank = jnp.sum(parts.astype(jnp.float32), axis=0).astype(jnp.bfloat16)
    gate_pre = contract_last(arrived, gate_weight[0])
    up_base = contract_last(arrived, up_weight[0])
    chosen = pick.astype(jnp.bfloat16)
    expanded = (rank[:, None, :] * chosen[:, :, None]).reshape(row_count, ADAPTERS * RANK)
    up = up_base + contract_last(expanded, adapter_out[0])
    hidden = (jax.nn.silu(gate_pre) * up).astype(jnp.bfloat16)
    down_w = down_weight[0]
    scattered = lax.psum_scatter(
        lax.dot_general(
            down_w, hidden, (((0,), (1,)), ((), ())), preferred_element_type=jnp.float32
        ).astype(jnp.bfloat16),
        "mp",
        scatter_dimension=0,
        tiled=True,
    )
    returned = lax.all_to_all(scattered, "expert", split_axis=1, concat_axis=1, tiled=True)
    returned_rows = jnp.transpose(returned)
    picked = returned_rows[slot_index].astype(jnp.float32)
    mixed = jnp.sum(route_gate[:, :, None] * picked, axis=1)
    return mixed.astype(jnp.bfloat16)


def solution(mesh):
    in_specs = (
        P("expert", "mp"),
        P("expert", None),
        P("expert", None),
        P(),
        P(),
        P(),
        P("expert", "mp", None),
        P("expert", "mp", None),
        P("expert", "mp", None),
        P("expert", "mp", None),
        P("expert", "mp", None),
    )
    out_specs = P("expert", "mp")
    return jax.shard_map(
        on_device, mesh=mesh, in_specs=in_specs, out_specs=out_specs, check_vma=False
    )
```

profile of v0, /device:TPU:2, one launch (start us, length us, event | category | flops | bytes accessed | tf_op | source)
XLA Modules:
  0.0 353.5 jit_solution(11466283499831162084)
XLA Ops:
  6.5 0.9 copy.63
  7.4 0.2 eq.77
  7.6 0.2 eq.73
  7.8 2.3 reduce-window.18
  10.1 0.3 slice_reduce_fusion
  10.3 0.2 reduce-window.19
  10.6 0.2 reduce_sum.87
  10.9 0.2 mul.96
  11.1 0.2 reshape.215
  11.3 4.3 %scatter_custom_fusion.1 = s32[2048]{0:T(1024)S(1)} fusion(s32[1024]{0:T(1024)S(1)} %bitcast.81, s32[1024]{0:T(1024)S(1)} %reshape.215, s32[]{:T(128)} %constant.14.clone.1), kind=kCustom, calls=%fused_computation.50 | custom fusion | bytes 8196 | tf_op jit(solution)/shard_map/scatter | solution.py:69
  15.6 0.9 select_reduce_fusion.2
  17.0 13.2 %gather_fusion.1 = s32[2048]{0:T(1024)S(1)} fusion(s32[512]{0:T(512)S(1)} %select_reduce_fusion, s32[2048]{0:T(1024)S(1)} %fusion.21), kind=kCustom, calls=%fused_computation.1 | custom fusion | bytes 24576 | tf_op jit(solution)/shard_map/gather | solution.py:71
  30.2 4.3 %scatter_custom_fusion = pred[2048]{0:T(1024)(128)(4,1)S(1)} fusion(s32[1024]{0:T(1024)S(1)} %bitcast.82, pred[1024]{0:T(1024)(128)(4,1)S(1)} %broadcast.114, pred[]{:T(512)} %constant.12.clone.1), kind=kCustom, calls=%fused_computation.52 | custom fusion | bytes 2049 | tf_op jit(solution)/shard_map/scatter | solution.py:70
  34.5 0.6 broadcast_select_fusion.1
  35.1 8.5 %all-to-all-start.2 = ((s32[8,256,1]{1,2,0:T(1,128)}), s32[8,256,1]{1,2,0:T(1,128)S(1)}, u32[]{:S(2)}, u32[]{:S(2)}) async-start(s32[8,256,1]{1,2,0:T(1,128)} %bitcast.9), calls=%async_computation.2 | async-start | bytes 16384 | tf_op jit(solution)/shard_map/all_to_all | solution.py:75
  43.8 6.2 %gather_fusion = bf16[2048,64]{1,0:T(8,128)(2,1)S(1)} fusion(bf16[512,64]{1,0:T(8,128)(2,1)S(1)} %copy.66, s32[2048]{0:T(1024)S(1)} %fusion.21), kind=kCustom, calls=%fused_computation | custom fusion | bytes 532480 | tf_op jit(solution)/shard_map/gather | solution.py:73
  49.9 0.2 copy.67
  50.2 0.2 all_to_all.34
  50.5 0.9 reshape.235
  51.4 7.6 %all-to-all-start.1 = ((bf16[32,2,1024]{2,1,0:T(2,128)(2,1)}), bf16[32,2,1024]{2,1,0:T(2,128)(2,1)S(1)}, u32[]{:S(2)}, u32[]{:S(2)}) async-start(bf16[32,2,1024]{2,1,0:T(2,128)(2,1)} %reshape.235), calls=%async_computation.1 | async-start | bytes 262144 | tf_op jit(solution)/shard_map/all_to_all | solution.py:60
  59.0 0.7 broadcast_select_fusion
  59.7 5.9 %all-to-all-done.1 = bf16[32,2,1024]{2,1,0:T(2,128)(2,1)S(1)} async-done(((bf16[32,2,1024]{2,1,0:T(2,128)(2,1)}), bf16[32,2,1024]{2,1,0:T(2,128)(2,1)S(1)}, u32[]{:S(2)}, u32[]{:S(2)}) %all-to-all-start.1) | async-done | bytes 131104 | tf_op jit(solution)/shard_map/all_to_all | solution.py:60
  65.6 7.2 %all-to-all-start = ((bf16[8,256,64]{1,2,0:T(8,128)(2,1)}), bf16[8,256,64]{1,2,0:T(8,128)(2,1)S(1)}, u32[]{:S(2)}, u32[]{:S(2)}) async-start(bf16[8,256,64]{1,2,0:T(8,128)(2,1)} %broadcast_select_fusion), calls=%async_computation | async-start | bytes 524288 | tf_op jit(solution)/shard_map/all_to_all | solution.py:74
  73.0 0.2 reshape.236
  73.2 11.8 %all-to-all-done = bf16[8,256,64]{1,2,0:T(8,128)(2,1)S(1)} async-done(((bf16[8,256,64]{1,2,0:T(8,128)(2,1)}), bf16[8,256,64]{1,2,0:T(8,128)(2,1)S(1)}, u32[]{:S(2)}, u32[]{:S(2)}) %all-to-all-start) | async-done | bytes 262176 | tf_op jit(solution)/shard_map/all_to_all | solution.py:74
  85.0 0.1 copy.68
  85.3 1.9 multiply_reduce_fusion
  87.3 0.7 copy.78
  88.0 0.2 reduce-scatter.4.cloned.1.call-start
  88.2 40.8 %all-gather.6.cloned.1.call-done = bf16[65536,16]{0,1:T(8,128)(2,1)} async-done(((bf16[2048,16]{0,1:T(8,128)(2,1)}), bf16[65536,16]{0,1:T(8,128)(2,1)}) %all-gather.6.cloned.1.call-update) | async-done | bytes 2097168 | tf_op jit(solution)/shard_map/all_gather | solution.py:85
  129.0 2.7 copy.80
  131.8 0.7 bitcast_reduce_fusion
  132.5 2.3 broadcast_multiply_fusion
  134.8 54.3 %all-gather.4.cloned.1.call-done = bf16[2048,2048]{0,1:T(8,128)(2,1)} async-done(((bf16[2048,64]{0,1:T(8,128)(2,1)}), bf16[2048,2048]{0,1:T(8,128)(2,1)}) %all-gather.4.cloned.1.call-update) | async-done | bytes 8388624 | tf_op jit(solution)/shard_map/all_gather | solution.py:84
  189.1 6.4 %fusion.6 = f32[2048,176]{0,1:T(8,128)} fusion(bf16[2048,2048]{0,1:T(8,128)(2,1)} %all-gather.4.cloned.1.call-done, bf16[1,176,2048]{2,1,0:T(8,128)(2,1)S(1)} %copy-done.5), kind=kOutput, calls=%fused_computation.17 | convolution fusion | flops 1476395008 | bytes 10551296 | tf_op jit(solution)/shard_map/dot_general | solution.py:35
  195.5 2.9 fusion.8
  198.4 9.7 %convert_bitcast_fusion = bf16[2048,2048]{0,1:T(8,128)(2,1)} fusion(f32[2048,176]{0,1:T(8,128)} %fusion.6, bf16[2048,1024]{0,1:T(8,128)(2,1)} %bitcast.69, f32[2048,176]{0,1:T(8,128)} %fusion.8, bf16[1,176,2048]{2,1,0:T(8,128)(2,1)S(1)} %copy-done, bf16[1,176,1024]{2,1,0:T(8,128)(2,1)S(1)} %copy-done.7), kind=kOutput, calls=%fused_computation.5 | convolution fusion | flops 2221309952 | bytes 16547840 | tf_op jit(solution)/shard_map/dot_general | solution.py:95
  208.0 12.3 %copy.76 = bf16[2048,2048]{1,0:T(8,128)(2,1)} copy(bf16[2048,2048]{0,1:T(8,128)(2,1)} %convert_bitcast_fusion) | data formatting | bytes 16777216
  220.4 99.9 %reduce-scatter.4.cloned.1.call-done = bf16[64,2048]{1,0:T(8,128)(2,1)} async-done(((bf16[2048,2048]{1,0:T(8,128)(2,1)}), bf16[64,2048]{1,0:T(8,128)(2,1)}) %reduce-scatter.4.cloned.1.call-update) | async-done | bytes 262160
  320.3 1.2 copy.77
  321.5 0.9 copy.73
  322.4 7.0 %all-to-all-start.3 = ((bf16[64,8,256]{2,0,1:T(8,128)(2,1)}), bf16[64,8,256]{2,0,1:T(8,128)(2,1)S(1)}, u32[]{:S(2)}, u32[]{:S(2)}) async-start(bf16[64,8,256]{2,0,1:T(8,128)(2,1)} %copy.73), calls=%async_computation.3 | async-start | bytes 524288 | tf_op jit(solution)/shard_map/all_to_all | solution.py:102
  329.4 0.2 reshape.197
  329.8 10.1 %all-to-all-done.3 = bf16[64,8,256]{2,0,1:T(8,128)(2,1)S(1)} async-done(((bf16[64,8,256]{2,0,1:T(8,128)(2,1)}), bf16[64,8,256]{2,0,1:T(8,128)(2,1)S(1)}, u32[]{:S(2)}, u32[]{:S(2)}) %all-to-all-start.3) | async-done | bytes 262176 | tf_op jit(solution)/shard_map/all_to_all | solution.py:102
  339.9 0.3 copy.74
  340.2 3.2 gather_fusion.2
  343.4 2.8 fusion.11
  346.3 0.7 copy.75
  (43 shorter events, 1.4 us)
Async XLA Ops:
  6.5 191.8 %copy-start = (bf16[1,176,2048]{2,1,0:T(8,128)(2,1)S(1)}, bf16[1,176,2048]{2,1,0:T(8,128)(2,1)}, u32[]{:S(2)}) copy-start(bf16[1,176,2048]{2,1,0:T(8,128)(2,1)} %param.19) | copy-start | bytes 2162692
  16.9 26.7 %copy-start.2 = (bf16[512,64]{0,1:T(8,128)(2,1)S(1)}, bf16[512,64]{0,1:T(8,128)(2,1)}, u32[]{:S(2)}) copy-start(bf16[512,64]{0,1:T(8,128)(2,1)} %param.11) | copy-start | bytes 196612
  30.2 20.0 %copy-start.1 = (bf16[1,32,2048]{2,1,0:T(8,128)(2,1)S(1)}, bf16[1,32,2048]{2,1,0:T(8,128)(2,1)}, u32[]{:S(2)}) copy-start(bf16[1,32,2048]{2,1,0:T(8,128)(2,1)} %param.20) | copy-start | bytes 393220
  35.1 16.2 %all-to-all-start.2 = ((s32[8,256,1]{1,2,0:T(1,128)}), s32[8,256,1]{1,2,0:T(1,128)S(1)}, u32[]{:S(2)}, u32[]{:S(2)}) async-start(s32[8,256,1]{1,2,0:T(1,128)} %bitcast.9), calls=%async_computation.2 | async-start | bytes 16384 | tf_op jit(solution)/shard_map/all_to_all | solution.py:75
  51.4 14.2 %all-to-all-start.1 = ((bf16[32,2,1024]{2,1,0:T(2,128)(2,1)}), bf16[32,2,1024]{2,1,0:T(2,128)(2,1)S(1)}, u32[]{:S(2)}, u32[]{:S(2)}) async-start(bf16[32,2,1024]{2,1,0:T(2,128)(2,1)} %reshape.235), calls=%async_computation.1 | async-start | bytes 262144 | tf_op jit(solution)/shard_map/all_to_all | solution.py:60
  65.6 19.4 %all-to-all-start = ((bf16[8,256,64]{1,2,0:T(8,128)(2,1)}), bf16[8,256,64]{1,2,0:T(8,128)(2,1)S(1)}, u32[]{:S(2)}, u32[]{:S(2)}) async-start(bf16[8,256,64]{1,2,0:T(8,128)(2,1)} %broadcast_select_fusion), calls=%async_computation | async-start | bytes 524288 | tf_op jit(solution)/shard_map/all_to_all | solution.py:74
  72.8 56.2 %all-gather.6.cloned.1.call-start = ((), (), s32[]{:S(2)}) async-start(), calls=%async_computation.6 | async-start | bytes 2162688 | tf_op jit(solution)/shard_map/all_gather | solution.py:85
  87.2 101.9 %all-gather.4.cloned.1.call-start = ((), (), s32[]{:S(2)}) async-start(), calls=%async_computation.5 | async-start | bytes 8650752 | tf_op jit(solution)/shard_map/all_gather | solution.py:84
  88.0 232.3 %reduce-scatter.4.cloned.1.call-start = ((), (), s32[]{:S(2)}) async-start(), calls=%async_computation.7 | async-start | bytes 8650752
  131.8 57.3 %copy-start.5 = (bf16[1,176,2048]{2,1,0:T(8,128)(2,1)S(1)}, bf16[1,176,2048]{2,1,0:T(8,128)(2,1)}, u32[]{:S(2)}) copy-start(bf16[1,176,2048]{2,1,0:T(8,128)(2,1)} %param.18) | copy-start | bytes 2162692
  134.8 60.7 %copy-start.6 = (bf16[1,176,2048]{2,1,0:T(8,128)(2,1)S(1)}, bf16[1,176,2048]{2,1,0:T(8,128)(2,1)}, u32[]{:S(2)}) copy-start(bf16[1,176,2048]{2,1,0:T(8,128)(2,1)} %param.17) | copy-start | bytes 2162692
  189.1 6.4 %copy-start.4 = (bf16[2048,2048]{0,1:T(8,128)(2,1)S(1)}, bf16[2048,2048]{0,1:T(8,128)(2,1)}, u32[]{:S(2)}) copy-start(bf16[2048,2048]{0,1:T(8,128)(2,1)} %all-gather.4.cloned.1.call-done) | copy-start | bytes 25165828
  195.5 2.9 copy-start.7
  220.4 109.2 %copy-start.3 = (f32[512,2]{0,1:T(2,128)S(1)}, f32[512,2]{0,1:T(2,128)}, u32[]{:S(2)}) copy-start(f32[512,2]{0,1:T(2,128)} %param.13) | copy-start | bytes 12292
  322.4 17.5 %all-to-all-start.3 = ((bf16[64,8,256]{2,0,1:T(8,128)(2,1)}), bf16[64,8,256]{2,0,1:T(8,128)(2,1)S(1)}, u32[]{:S(2)}, u32[]{:S(2)}) async-start(bf16[64,8,256]{2,0,1:T(8,128)(2,1)} %copy.73), calls=%async_computation.3 | async-start | bytes 524288 | tf_op jit(solution)/shard_map/all_to_all | solution.py:102
Sparse Core Ops, SparseCore 0:
  87.3 41.6 all-gather.5
  131.6 57.4 all-gather.3
  220.5 99.7 reduce-scatter.3
where the time goes:
time: 354 us
  waiting for transfers between devices  223 us (63%)
  local copies, waits for them, and re-layouts  54.8 us (15%)
  starting transfers between devices  30.6 us (9%)
  matrix products  20.8 us (6%)
  between operations  13.4 us (4%)
  other arithmetic  11.1 us (3%)
    unnamed x4, waiting for transfers between devices  99.9 us
    all_gather x1, waiting for transfers between devices, on_device(): arrived = lax.all_gather(arrived_local, 'mp', axis=1, tiled=True)  54.3 us
    all_gather x1, waiting for transfers between devices, on_device(): lax.all_gather(part_rank.astype(jnp.bfloat16), 'mp', axis=0, tiled=False)  40.8 us
    unnamed x24, local copies, waits for them, and re-layouts  18.6 us
    gather x1, local copies, waits for them, and re-layouts, on_device(): slot_adapter = jnp.where(filled, adapter_of[slot_token], -1)  13.2 us
    all_to_all x1, waiting for transfers between devices, on_device(): lax.all_to_all(send_rows, 'expert', split_axis=0, concat_axis=0, tiled=True)  11.8 us
    dot_general x3, matrix products, contract_last(): lax.dot_general(left, right, (((1,), (1,)), ((), ())), preferred_element_...  11.1 us
    all_to_all x1, waiting for transfers between devices, on_device(): lax.all_to_all(scattered, 'expert', split_axis=1, concat_axis=1, tiled=True)  10.1 us
  transfers between devices with their start and end apart: 7, of which 6 were waited for; matrix products, arithmetic and copies ran while one was open for 4% of the time, Pallas kernels for 0%

commit v1 on v0

--- a/solution.py
+++ b/solution.py
@@ -81,7 +81,9 @@
         jnp.float32
     )
     part_rank = jnp.sum(part_all.reshape(row_count, ADAPTERS, RANK) * pick[:, :, None], axis=1)
-    arrived = lax.all_gather(arrived_local, "mp", axis=1, tiled=True)
+    arrived = jnp.concatenate(
+        lax.all_to_all(jnp.stack([arrived_local] * lax.axis_size("mp")), "mp", 0, 0), axis=1
+    )
     parts = lax.all_gather(part_rank.astype(jnp.bfloat16), "mp", axis=0, tiled=False)
     rank = jnp.sum(parts.astype(jnp.float32), axis=0).astype(jnp.bfloat16)
     gate_pre = contract_last(arrived, gate_weight[0])

time: 354 us -> 384 us (1.085)
  waiting for transfers between devices: 223 us -> 242 us
  starting transfers between devices: 30.6 us -> 36.1 us
    all_gather x1, waiting for transfers between devices: 40.8 us -> 107 us  [on_device(): lax.all_gather(part_rank.astype(jnp.bfloat16), 'mp', axis=0, tiled=False)]
    all_gather x1 -> x0, waiting for transfers between devices: 54.3 us -> none  [on_device(): arrived = lax.all_gather(arrived_local, 'mp', axis=1, tiled=True)]
    unnamed x4 -> x3, waiting for transfers between devices: 99.9 us -> 107 us
    all_to_all x0 -> x1, starting transfers between devices: none -> 6.04 us  [on_device(): lax.all_to_all(jnp.stack([arrived_local] * lax.axis_size('mp')), 'mp', 0, 0)]
    another operation x1 -> x4, local copies, waits for them, and re-layouts: 0.09 us -> 4.51 us  [the longest x3 4.42 us: on_device(): jnp.stack([arrived_local] * lax.axis_size('mp'))]
    unnamed x24 -> x22, local copies, waits for them, and re-layouts: 18.6 us -> 18.6 us
where the time goes in v1:
time: 384 us
  waiting for transfers between devices  242 us (63%)
  local copies, waits for them, and re-layouts  58.3 us (15%)
  starting transfers between devices  36.1 us (9%)
  matrix products  22.5 us (6%)
  between operations  13.7 us (4%)
  other arithmetic  11 us (3%)
    unnamed x3, waiting for transfers between devices  107 us
    all_gather x1, waiting for transfers between devices, on_device(): lax.all_gather(part_rank.astype(jnp.bfloat16), 'mp', axis=0, tiled=False)  107 us
    unnamed x22, local copies, waits for them, and re-layouts  18.6 us
    dot_general x3, matrix products, contract_last(): lax.dot_general(left, right, (((1,), (1,)), ((), ())), preferred_element_...  13.3 us
    gather x1, local copies, waits for them, and re-layouts, on_device(): slot_adapter = jnp.where(filled, adapter_of[slot_token], -1)  13.2 us
    all_to_all x1, waiting for transfers between devices, on_device(): lax.all_to_all(scattered, 'expert', split_axis=1, concat_axis=1, tiled=True)  10.1 us
    all_to_all x1, waiting for transfers between devices, on_device(): lax.all_to_all(send_rows, 'expert', split_axis=0, concat_axis=0, tiled=True)  10.1 us
    dot_general x1, matrix products, on_device(): lax.dot_general(down_w, hidden, (((0,), (1,)), ((), ())), preferred_eleme...  9.23 us
  transfers between devices with their start and end apart: 7, of which 6 were waited for; matrix products, arithmetic and copies ran while one was open for 4% of the time, Pallas kernels for 0%

profile of v1, /device:TPU:2, one launch (start us, length us, event | category | flops | bytes accessed | tf_op | source)
XLA Modules:
  0.0 383.5 jit_solution(14239159502898504249)
XLA Ops:
  6.5 0.9 copy.64
  7.4 0.2 eq.77
  7.6 0.2 eq.73
  7.8 2.3 reduce-window.18
  10.1 0.3 slice_reduce_fusion
  10.3 0.2 reduce-window.19
  10.6 0.2 reduce_sum.87
  10.9 0.2 mul.96
  11.1 0.2 reshape.226
  11.3 4.3 %scatter_custom_fusion.1 = s32[2048]{0:T(1024)S(1)} fusion(s32[1024]{0:T(1024)S(1)} %bitcast.84, s32[1024]{0:T(1024)S(1)} %reshape.226, s32[]{:T(128)} %constant.14.clone.1), kind=kCustom, calls=%fused_computation.50 | custom fusion | bytes 8196 | tf_op jit(solution)/shard_map/scatter | solution.py:69
  15.6 0.9 select_reduce_fusion.2
  16.8 4.3 %scatter_custom_fusion = pred[2048]{0:T(1024)(128)(4,1)S(1)} fusion(s32[1024]{0:T(1024)S(1)} %bitcast.85, pred[1024]{0:T(1024)(128)(4,1)S(1)} %broadcast.115, pred[]{:T(512)} %constant.12.clone.1), kind=kCustom, calls=%fused_computation.52 | custom fusion | bytes 2049 | tf_op jit(solution)/shard_map/scatter | solution.py:70
  21.3 13.2 %gather_fusion.1 = s32[2048]{0:T(1024)S(1)} fusion(s32[512]{0:T(512)S(1)} %select_reduce_fusion, s32[2048]{0:T(1024)S(1)} %fusion.21), kind=kCustom, calls=%fused_computation.1 | custom fusion | bytes 24576 | tf_op jit(solution)/shard_map/gather | solution.py:71
  34.5 0.6 broadcast_select_fusion.1
  35.1 8.5 %all-to-all-start.3 = ((s32[8,256,1]{1,2,0:T(1,128)}), s32[8,256,1]{1,2,0:T(1,128)S(1)}, u32[]{:S(2)}, u32[]{:S(2)}) async-start(s32[8,256,1]{1,2,0:T(1,128)} %bitcast.12), calls=%async_computation.3 | async-start | bytes 16384 | tf_op jit(solution)/shard_map/all_to_all | solution.py:75
  43.8 6.2 %gather_fusion = bf16[2048,64]{1,0:T(8,128)(2,1)S(1)} fusion(bf16[512,64]{1,0:T(8,128)(2,1)S(1)} %copy.67, s32[2048]{0:T(1024)S(1)} %fusion.21), kind=kCustom, calls=%fused_computation | custom fusion | bytes 532480 | tf_op jit(solution)/shard_map/gather | solution.py:73
  49.9 0.2 copy.68
  50.1 0.7 broadcast_select_fusion
  50.9 0.5 all-to-all-done.3
  51.3 6.7 %all-to-all-start = ((bf16[8,256,64]{1,2,0:T(8,128)(2,1)}), bf16[8,256,64]{1,2,0:T(8,128)(2,1)S(1)}, u32[]{:S(2)}, u32[]{:S(2)}) async-start(bf16[8,256,64]{1,2,0:T(8,128)(2,1)} %broadcast_select_fusion), calls=%async_computation | async-start | bytes 524288 | tf_op jit(solution)/shard_map/all_to_all | solution.py:74
  58.1 0.2 all_to_all.35
  58.4 0.9 reshape.246
  59.3 10.1 %all-to-all-done = bf16[8,256,64]{1,2,0:T(8,128)(2,1)S(1)} async-done(((bf16[8,256,64]{1,2,0:T(8,128)(2,1)}), bf16[8,256,64]{1,2,0:T(8,128)(2,1)S(1)}, u32[]{:S(2)}, u32[]{:S(2)}) %all-to-all-start) | async-done | bytes 262176 | tf_op jit(solution)/shard_map/all_to_all | solution.py:74
  69.4 7.6 %all-to-all-start.2 = ((bf16[32,2,1024]{2,1,0:T(2,128)(2,1)}), bf16[32,2,1024]{2,1,0:T(2,128)(2,1)S(1)}, u32[]{:S(2)}, u32[]{:S(2)}) async-start(bf16[32,2,1024]{2,1,0:T(2,128)(2,1)} %reshape.246), calls=%async_computation.2 | async-start | bytes 262144 | tf_op jit(solution)/shard_map/all_to_all | solution.py:60
  77.0 6.6 %all-to-all-done.2 = bf16[32,2,1024]{2,1,0:T(2,128)(2,1)S(1)} async-done(((bf16[32,2,1024]{2,1,0:T(2,128)(2,1)}), bf16[32,2,1024]{2,1,0:T(2,128)(2,1)S(1)}, u32[]{:S(2)}, u32[]{:S(2)}) %all-to-all-start.2) | async-done | bytes 131104 | tf_op jit(solution)/shard_map/all_to_all | solution.py:60
  83.6 4.3 %stack.5 = bf16[32,2048,64]{1,2,0:T(8,128)(2,1)} broadcast(bf16[2048,64]{0,1:T(8,128)(2,1)S(1)} %bitcast.77), dimensions={1,2} | broadcast | bytes 8650752 | tf_op jit(solution)/shard_map/stack | solution.py:85
  87.9 6.0 %all-to-all-start.1 = ((bf16[32,2048,64]{1,2,0:T(8,128)(2,1)}), bf16[32,2048,64]{1,2,0:T(8,128)(2,1)}, u32[]{:S(2)}, u32[]{:S(2)}) async-start(bf16[32,2048,64]{1,2,0:T(8,128)(2,1)} %stack.5), calls=%async_computation.1 | async-start | bytes 16777216 | tf_op jit(solution)/shard_map/all_to_all | solution.py:85
  94.1 0.2 reshape.247
  94.6 1.9 multiply_reduce_fusion
  96.5 0.2 reduce-scatter.4.cloned.1.call-start
  96.7 107.2 %all-gather.3.cloned.1.call-done = bf16[65536,16]{0,1:T(8,128)(2,1)} async-done(((bf16[2048,16]{0,1:T(8,128)(2,1)}), bf16[65536,16]{0,1:T(8,128)(2,1)}) %all-gather.3.cloned.1.call-update) | async-done | bytes 2097168 | tf_op jit(solution)/shard_map/all_gather | solution.py:87
  204.0 2.7 copy.81
  206.7 0.7 bitcast_reduce_fusion
  207.4 2.3 broadcast_multiply_fusion
  209.7 5.1 %fusion.6 = f32[2048,176]{0,1:T(8,128)S(1)} fusion(bf16[2048,2048]{0,1:T(8,128)(2,1)} %bitcast.5, bf16[1,176,2048]{2,1,0:T(8,128)(2,1)S(1)} %copy-done.4), kind=kOutput, calls=%fused_computation.17 | convolution fusion | flops 1476395008 | bytes 10551296 | tf_op jit(solution)/shard_map/dot_general | solution.py:35
  214.8 6.3 %fusion.8 = f32[2048,176]{0,1:T(8,128)} fusion(bf16[2048,2048]{0,1:T(8,128)(2,1)} %bitcast.5, bf16[1,176,2048]{2,1,0:T(8,128)(2,1)S(1)} %copy-done.5), kind=kOutput, calls=%fused_computation.19 | convolution fusion | flops 1476395008 | bytes 10551296 | tf_op jit(solution)/shard_map/dot_general | solution.py:35
  221.2 9.2 %convert_bitcast_fusion = bf16[2048,2048]{0,1:T(8,128)(2,1)} fusion(f32[2048,176]{0,1:T(8,128)S(1)} %fusion.6, bf16[2048,1024]{0,1:T(8,128)(2,1)} %bitcast.72, f32[2048,176]{0,1:T(8,128)} %fusion.8, bf16[1,176,2048]{2,1,0:T(8,128)(2,1)S(1)} %copy-done, bf16[1,176,1024]{2,1,0:T(8,128)(2,1)S(1)} %copy-done.6), kind=kOutput, calls=%fused_computation.5 | convolution fusion | flops 2221309952 | bytes 16547840 | tf_op jit(solution)/shard_map/dot_general | solution.py:97
  230.4 12.3 %copy.77 = bf16[2048,2048]{1,0:T(8,128)(2,1)} copy(bf16[2048,2048]{0,1:T(8,128)(2,1)} %convert_bitcast_fusion) | data formatting | bytes 16777216
  242.8 107.2 %reduce-scatter.4.cloned.1.call-done = bf16[64,2048]{1,0:T(8,128)(2,1)} async-done(((bf16[2048,2048]{1,0:T(8,128)(2,1)}), bf16[64,2048]{1,0:T(8,128)(2,1)}) %reduce-scatter.4.cloned.1.call-update) | async-done | bytes 262160
  350.0 1.2 copy.78
  351.2 0.9 copy.74
  352.1 7.0 %all-to-all-start.4 = ((bf16[64,8,256]{2,0,1:T(8,128)(2,1)}), bf16[64,8,256]{2,0,1:T(8,128)(2,1)S(1)}, u32[]{:S(2)}, u32[]{:S(2)}) async-start(bf16[64,8,256]{2,0,1:T(8,128)(2,1)} %copy.74), calls=%async_computation.4 | async-start | bytes 524288 | tf_op jit(solution)/shard_map/all_to_all | solution.py:104
  359.1 0.2 reshape.208
  359.5 10.1 %all-to-all-done.4 = bf16[64,8,256]{2,0,1:T(8,128)(2,1)S(1)} async-done(((bf16[64,8,256]{2,0,1:T(8,128)(2,1)}), bf16[64,8,256]{2,0,1:T(8,128)(2,1)S(1)}, u32[]{:S(2)}, u32[]{:S(2)}) %all-to-all-start.4) | async-done | bytes 262176 | tf_op jit(solution)/shard_map/all_to_all | solution.py:104
  369.6 0.3 copy.75
  369.9 3.2 gather_fusion.2
  373.1 2.8 fusion.11
  376.0 0.7 copy.76
  (41 shorter events, 1.5 us)
Async XLA Ops:
  6.5 214.6 %copy-start = (bf16[1,176,2048]{2,1,0:T(8,128)(2,1)S(1)}, bf16[1,176,2048]{2,1,0:T(8,128)(2,1)}, u32[]{:S(2)}) copy-start(bf16[1,176,2048]{2,1,0:T(8,128)(2,1)} %param.19) | copy-start | bytes 2162692
  21.3 22.3 %copy-start.2 = (bf16[512,64]{0,1:T(8,128)(2,1)S(1)}, bf16[512,64]{0,1:T(8,128)(2,1)}, u32[]{:S(2)}) copy-start(bf16[512,64]{0,1:T(8,128)(2,1)} %param.11) | copy-start | bytes 196612
  34.5 23.5 %copy-start.1 = (bf16[1,32,2048]{2,1,0:T(8,128)(2,1)S(1)}, bf16[1,32,2048]{2,1,0:T(8,128)(2,1)}, u32[]{:S(2)}) copy-start(bf16[1,32,2048]{2,1,0:T(8,128)(2,1)} %param.20) | copy-start | bytes 393220
  35.1 16.2 %all-to-all-start.3 = ((s32[8,256,1]{1,2,0:T(1,128)}), s32[8,256,1]{1,2,0:T(1,128)S(1)}, u32[]{:S(2)}, u32[]{:S(2)}) async-start(s32[8,256,1]{1,2,0:T(1,128)} %bitcast.12), calls=%async_computation.3 | async-start | bytes 16384 | tf_op jit(solution)/shard_map/all_to_all | solution.py:75
  51.3 18.1 %all-to-all-start = ((bf16[8,256,64]{1,2,0:T(8,128)(2,1)}), bf16[8,256,64]{1,2,0:T(8,128)(2,1)S(1)}, u32[]{:S(2)}, u32[]{:S(2)}) async-start(bf16[8,256,64]{1,2,0:T(8,128)(2,1)} %broadcast_select_fusion), calls=%async_computation | async-start | bytes 524288 | tf_op jit(solution)/shard_map/all_to_all | solution.py:74
  69.4 14.2 %all-to-all-start.2 = ((bf16[32,2,1024]{2,1,0:T(2,128)(2,1)}), bf16[32,2,1024]{2,1,0:T(2,128)(2,1)S(1)}, u32[]{:S(2)}, u32[]{:S(2)}) async-start(bf16[32,2,1024]{2,1,0:T(2,128)(2,1)} %reshape.246), calls=%async_computation.2 | async-start | bytes 262144 | tf_op jit(solution)/shard_map/all_to_all | solution.py:60
  87.9 121.8 %all-to-all-start.1 = ((bf16[32,2048,64]{1,2,0:T(8,128)(2,1)}), bf16[32,2048,64]{1,2,0:T(8,128)(2,1)}, u32[]{:S(2)}, u32[]{:S(2)}) async-start(bf16[32,2048,64]{1,2,0:T(8,128)(2,1)} %stack.5), calls=%async_computation.1 | async-start | bytes 16777216 | tf_op jit(solution)/shard_map/all_to_all | solution.py:85
  94.0 110.0 %all-gather.3.cloned.1.call-start = ((), (), s32[]{:S(2)}) async-start(), calls=%async_computation.6 | async-start | bytes 2162688 | tf_op jit(solution)/shard_map/all_gather | solution.py:87
  96.5 253.5 %reduce-scatter.4.cloned.1.call-start = ((), (), s32[]{:S(2)}) async-start(), calls=%async_computation.7 | async-start | bytes 8650752
  206.7 3.0 copy-start.4
  209.7 5.1 %copy-start.5 = (bf16[1,176,2048]{2,1,0:T(8,128)(2,1)S(1)}, bf16[1,176,2048]{2,1,0:T(8,128)(2,1)}, u32[]{:S(2)}) copy-start(bf16[1,176,2048]{2,1,0:T(8,128)(2,1)} %param.17) | copy-start | bytes 2162692
  214.8 6.3 %copy-start.6 = (bf16[1,176,1024]{2,1,0:T(8,128)(2,1)S(1)}, bf16[1,176,1024]{2,1,0:T(8,128)(2,1)}, u32[]{:S(2)}) copy-start(bf16[1,176,1024]{2,1,0:T(8,128)(2,1)} %param.21) | copy-start | bytes 1081348
  242.7 116.6 %copy-start.3 = (f32[512,2]{0,1:T(2,128)S(1)}, f32[512,2]{0,1:T(2,128)}, u32[]{:S(2)}) copy-start(f32[512,2]{0,1:T(2,128)} %param.13) | copy-start | bytes 12292
  352.1 17.5 %all-to-all-start.4 = ((bf16[64,8,256]{2,0,1:T(8,128)(2,1)}), bf16[64,8,256]{2,0,1:T(8,128)(2,1)S(1)}, u32[]{:S(2)}, u32[]{:S(2)}) async-start(bf16[64,8,256]{2,0,1:T(8,128)(2,1)} %copy.74), calls=%async_computation.4 | async-start | bytes 524288 | tf_op jit(solution)/shard_map/all_to_all | solution.py:104
Sparse Core Ops, SparseCore 0:
  97.4 106.5 all-gather.2
  242.9 107.0 reduce-scatter.3
